TPU v7x, 512 devices: a whole 4x4x16 slice. The times are simulated.
512 devices in a mesh: req: 32 (over y, x, core), mlp: 16 (over z).
Axes of the slice: x: 4, y: 4, z: 16, core: 2. Of those that a mesh axis runs over, the one named last changes fastest.
Arguments:
- queries: bfloat16 [12288, 4096], P('req', 'mlp')
- new_keys: bfloat16 [12288, 1024], P(('req', 'mlp')), may hold values from -5 to 5
- new_values: bfloat16 [12288, 1024], P(('req', 'mlp')), may hold values from -6 to 6
- cache_keys: bfloat16 [32, 4096, 1024], P('req', 'mlp')
- cache_values: bfloat16 [32, 4096, 1024], P('req', 'mlp'), may hold values from -6 to 6
- cache_len: int32 [32], P('req'), may hold values from 256 to 4096, as said below
- residual: bfloat16 [12288, 2560], P('req')
- out_weight: bfloat16 [4096, 2560], P('mlp'), may hold values from -0.1796875 to 0.1796875
- norm_gain: bfloat16 [2560], replicated, may hold values from 0.099609375 to 1.8984375
- gate_weight: bfloat16 [2560, 9728], P('req', 'mlp'), may hold values from -0.125 to 0.125
- up_weight: bfloat16 [2560, 9728], P('req', 'mlp'), may hold values from -0.125 to 0.125
- down_weight: bfloat16 [2560, 9728], P('req', 'mlp'), may hold values from -0.0625 to 0.0625
Outputs:
- layer_out: bfloat16 [12288, 2560], P(('req', 'mlp'))
Inputs may be any that keep to these rules, and one draw needn't show every extreme that they name: cache_len[r] counts request r's valid cached positions from the first; some request has exactly 4096.
All inputs are finite; a program needn't handle non-finite values.
Results may differ from a plain program's by a relative error of at most 0.012.
Values may be sent and summed in bfloat16 or wider, within the bound.
No kernel may reach another device: no remote copies, remote signals or barrier semaphores. Data moves between devices by JAX's collectives and lax.ppermute only.
A program may use at most 64 MiB of HBM per device.

v0:
```python
import jax
import jax.numpy as jnp
from jax import lax
from jax.sharding import PartitionSpec as P

H = 32
KVH = 8
HD = 128
norm_eps = 1e-06


def shards(
    queries,
    new_keys,
    new_values,
    cache_keys,
    cache_values,
    cache_len,
    residual,
    out_weight,
    norm_gain,
    gate_weight,
    up_weight,
    down_weight,
):
    n_mlp = lax.axis_size("mlp")
    heads_dev = H // n_mlp
    group_size = H // KVH
    kv_dev = max(1, heads_dev // group_size)
    per_kv = heads_dev // kv_dev
    query_rows = queries.shape[0]
    rows_dev = new_keys.shape[0]
    cache_total = cache_keys.shape[1] * n_mlp

    def to_slots(rows_block):
        row_count = rows_block.shape[0]
        copies = n_mlp // KVH
        spread = jnp.broadcast_to(
            rows_block.reshape(row_count, KVH, 1, HD), (row_count, KVH, copies, HD)
        )
        return spread.reshape(row_count, n_mlp, HD)

    arrived = (
        lax.all_to_all(to_slots(cache_keys[0]), "mlp", split_axis=1, concat_axis=0, tiled=True),
        lax.all_to_all(to_slots(cache_values[0]), "mlp", split_axis=1, concat_axis=0, tiled=True),
        lax.all_to_all(to_slots(new_keys), "mlp", split_axis=1, concat_axis=0, tiled=True),
        lax.all_to_all(to_slots(new_values), "mlp", split_axis=1, concat_axis=0, tiled=True),
    )
    keys_old = arrived[0]
    values_old = arrived[1]
    keys_new = arrived[2]
    values_new = arrived[3]
    grouped = queries.reshape(query_rows, kv_dev, per_kv, HD)
    score_scale = HD ** (-0.5)

    def absorb(running, key_part, value_part, allowed):
        row_max, row_sum, weighted = running
        scores = (
            jnp.einsum("tgqd,kgd->gqtk", grouped, key_part, preferred_element_type=jnp.float32)
            * score_scale
        )
        scores = jnp.where(allowed, scores, -jnp.inf)
        new_max = jnp.maximum(row_max, jnp.max(scores, axis=-1))
        shrink = jnp.exp(row_max - new_max)
        weights = jnp.exp(scores - new_max[..., None])
        row_sum = row_sum * shrink + jnp.sum(weights, axis=-1)
        weighted = weighted * shrink[..., None] + jnp.einsum(
            "gqtk,kgd->gqtd",
            weights.astype(jnp.bfloat16),
            value_part,
            preferred_element_type=jnp.float32,
        )
        return (new_max, row_sum, weighted)

    start_state = (
        jnp.full((kv_dev, per_kv, query_rows), -jnp.inf, jnp.float32),
        jnp.zeros((kv_dev, per_kv, query_rows), jnp.float32),
        jnp.zeros((kv_dev, per_kv, query_rows, HD), jnp.float32),
    )
    token_ids = lax.iota(jnp.int32, query_rows)
    causal = token_ids[None, :] <= token_ids[:, None]
    running = absorb(start_state, keys_new, values_new, causal)
    length = cache_len[0]
    key_block = min(512, cache_total)

    def visit(turn_index, running):
        offset = turn_index * key_block
        key_part = lax.dynamic_slice_in_dim(keys_old, offset, key_block, 0)
        value_part = lax.dynamic_slice_in_dim(values_old, offset, key_block, 0)
        positions = offset + lax.iota(jnp.int32, key_block)
        return absorb(running, key_part, value_part, (positions < length)[None, :])

    block_count = cache_total // key_block
    row_max, row_sum, weighted = lax.fori_loop(0, block_count, visit, running)
    attended = (weighted / row_sum[..., None]).astype(jnp.bfloat16)
    attended = attended.transpose(2, 0, 1, 3).reshape(query_rows, heads_dev * HD)
    partial_value = jnp.dot(attended, out_weight, preferred_element_type=jnp.float32)
    row_start = lax.axis_index("mlp") * rows_dev
    head_sum = lax.psum(partial_value.astype(jnp.bfloat16), "mlp").astype(jnp.float32)
    stream = (residual.astype(jnp.float32) + head_sum).astype(jnp.bfloat16)
    stream_full = stream.astype(jnp.float32)
    factor = lax.rsqrt(jnp.mean(stream_full * stream_full, axis=-1, keepdims=True) + norm_eps)
    normed = (stream_full * factor * norm_gain.astype(jnp.float32)).astype(jnp.bfloat16)
    stream_rows = lax.dynamic_slice_in_dim(stream, row_start, rows_dev, 0)
    gate_sum = jnp.dot(
        normed,
        lax.all_gather(gate_weight, "req", axis=0, tiled=True),
        preferred_element_type=jnp.float32,
    )
    up_sum = jnp.dot(
        normed,
        lax.all_gather(up_weight, "req", axis=0, tiled=True),
        preferred_element_type=jnp.float32,
    )
    hidden = (jax.nn.silu(gate_sum) * up_sum).astype(jnp.bfloat16)
    mlp_part = lax.dot_general(
        hidden,
        lax.all_gather(down_weight, "req", axis=0, tiled=True),
        (((1,), (1,)), ((), ())),
        preferred_element_type=jnp.float32,
    )
    mlp_rows = lax.psum_scatter(
        mlp_part.astype(jnp.bfloat16), "mlp", scatter_dimension=0, tiled=True
    ).astype(jnp.float32)
    return (stream_rows.astype(jnp.float32) + mlp_rows).astype(jnp.bfloat16)


def solution(mesh):
    in_specs = (
        P("req", "mlp"),
        P(("req", "mlp"), None),
        P(("req", "mlp"), None),
        P("req", "mlp", None),
        P("req", "mlp", None),
        P("req"),
        P("req", None),
        P("mlp", None),
        P(),
        P("req", "mlp"),
        P("req", "mlp"),
        P("req", "mlp"),
    )
    out_specs = P(("req", "mlp"), None)
    return jax.shard_map(shards, mesh=mesh, in_specs=in_specs, out_specs=out_specs, check_vma=False)
```

profile of v0, /device:TPU:2, one launch (start us, length us, event | category | flops | bytes accessed | tf_op | source)
XLA Modules:
  0.0 472.2 jit_solution(10438826310127697672)
XLA Ops:
  7.4 0.9 copy_bitcast_fusion.1
  8.3 0.7 broadcast_in_dim.89
  8.9 15.2 %all-to-all-start = ((bf16[24,16,128]{2,0,1:T(8,128)(2,1)}), bf16[24,16,128]{2,0,1:T(8,128)(2,1)S(1)}, u32[]{:S(2)}, u32[]{:S(2)}) async-start(bf16[24,16,128]{2,0,1:T(8,128)(2,1)} %bitcast.13), calls=%async_computation | async-start | bytes 196608 | tf_op jit(solution)/shard_map/all_to_all | solution.py:46
  24.1 0.8 copy_bitcast_fusion
  25.0 12.7 %all-to-all-done = bf16[24,16,128]{2,0,1:T(8,128)(2,1)S(1)} async-done(((bf16[24,16,128]{2,0,1:T(8,128)(2,1)}), bf16[24,16,128]{2,0,1:T(8,128)(2,1)S(1)}, u32[]{:S(2)}, u32[]{:S(2)}) %all-to-all-start) | async-done | bytes 98336 | tf_op jit(solution)/shard_map/all_to_all | solution.py:46
  37.7 0.7 broadcast_in_dim.96
  38.4 3.6 all-to-all-start.1
  41.9 1.1 copy.35
  43.2 11.9 %all-to-all-done.1 = bf16[24,16,128]{2,0,1:T(8,128)(2,1)S(1)} async-done(((bf16[24,16,128]{2,0,1:T(8,128)(2,1)}), bf16[24,16,128]{2,0,1:T(8,128)(2,1)S(1)}, u32[]{:S(2)}, u32[]{:S(2)}) %all-to-all-start.1) | async-done | bytes 98336 | tf_op jit(solution)/shard_map/all_to_all | solution.py:47
  55.1 1.2 broadcast_in_dim.98
  56.3 3.7 all-to-all-start.2
  60.1 48.7 %all-to-all-done.2 = bf16[256,16,128]{2,0,1:T(8,128)(2,1)S(1)} async-done(((bf16[256,16,128]{2,0,1:T(8,128)(2,1)}), bf16[256,16,128]{2,0,1:T(8,128)(2,1)S(1)}, u32[]{:S(2)}, u32[]{:S(2)}) %all-to-all-start.2) | async-done | bytes 1048608 | tf_op jit(solution)/shard_map/all_to_all | solution.py:44
  108.9 1.3 broadcast_in_dim.100
  110.2 7.9 %all-to-all-start.3 = ((bf16[256,16,128]{2,0,1:T(8,128)(2,1)}), bf16[256,16,128]{2,0,1:T(8,128)(2,1)S(1)}, u32[]{:S(2)}, u32[]{:S(2)}) async-start(bf16[256,16,128]{2,0,1:T(8,128)(2,1)} %bitcast.35), calls=%async_computation.3 | async-start | bytes 2097152 | tf_op jit(solution)/shard_map/all_to_all | solution.py:45
  119.5 48.7 %all-to-all-done.3 = bf16[256,16,128]{2,0,1:T(8,128)(2,1)S(1)} async-done(((bf16[256,16,128]{2,0,1:T(8,128)(2,1)}), bf16[256,16,128]{2,0,1:T(8,128)(2,1)S(1)}, u32[]{:S(2)}, u32[]{:S(2)}) %all-to-all-start.3) | async-done | bytes 1048608 | tf_op jit(solution)/shard_map/all_to_all | solution.py:45
  168.2 22.4 %while.17 = (s32[]{:T(128)}, f32[1,2,384]{2,1,0:T(2,128)S(1)}, f32[1,2,384]{2,1,0:T(2,128)S(1)}, f32[1,2,384,128]{3,2,1,0:T(8,128)S(1)}, s32[]{:T(128)}, /*index...) while((s32[]{:T(128)}, f32[1,2,384]{2,1,0:T(2,128)S(1)}, ...), condition=%wide.region_5.6_spmd, body=%wide.region_2.5_spmd.sunk | while | flops 204279040 | bytes 6014131 | solution.py:94
  168.8 1.3 bitcast_reduce_fusion.2
  171.7 1.3 bitcast_reduce_fusion.2
  174.5 1.3 bitcast_reduce_fusion.2
  177.3 1.3 bitcast_reduce_fusion.2
  180.1 1.3 bitcast_reduce_fusion.2
  182.9 1.3 bitcast_reduce_fusion.2
  185.7 1.3 bitcast_reduce_fusion.2
  188.5 1.3 bitcast_reduce_fusion.2
  190.8 2.1 convolution_convert_fusion.1
  194.8 139.0 %all-reduce.2.cloned.1.call-done = bf16[384,2560]{1,0:T(8,128)(2,1)} async-done(((bf16[384,2560]{1,0:T(8,128)(2,1)}), bf16[384,2560]{1,0:T(8,128)(2,1)}) %all-reduce.2.cloned.1.call-update) | async-done | bytes 1966096 | tf_op jit(solution)/shard_map/psum | solution.py:99
  333.8 3.0 fusion.15
  336.8 4.8 %fusion.29 = f32[384,608]{0,1:T(8,128)} fusion(bf16[2560,608]{1,0:T(8,128)(2,1)} %all-gather.4.cloned.1.call-done, bf16[384,2560]{1,0:T(8,128)(2,1)S(1)} %get-tuple-element.174, f32[2560]{0:T(1024)S(1)} %convert_element_type.57, f32[384]{0:T(512)S(1)} %add_rsqrt_fusion), kind=kOutput, calls=%fused_computation.43 | convolution fusion | flops 1199308800 | bytes 6024704 | tf_op jit(solution)/shard_map/dot_general | solution.py:105
  341.6 40.2 %all-gather.8.cloned.1.call-done = bf16[2560,608]{1,0:T(8,128)(2,1)} async-done(((bf16[80,608]{1,0:T(8,128)(2,1)}), bf16[2560,608]{1,0:T(8,128)(2,1)}) %all-gather.8.cloned.1.call-update) | async-done | bytes 3112976 | tf_op jit(solution)/shard_map/all_gather | solution.py:118
  381.8 8.1 %convolution_convert_fusion = bf16[384,2560]{1,0:T(8,128)(2,1)} fusion(bf16[2560,608]{1,0:T(8,128)(2,1)} %all-gather.8.cloned.1.call-done, bf16[2560,608]{1,0:T(8,128)(2,1)} %all-gather.6.cloned.1.call-done, f32[384,608]{0,1:T(8,128)} %fusion.29, bf16[384,2560]{1,0:T(8,128)(2,1)S(1)} %get-tuple-element.174, f32[2560]{0:T(1024)S(1)} %convert_element_type.57, ...), kind=kOutput, calls=%fused_computation.24 | convolution fusion | flops 2397069312 | bytes 11103744 | tf_op jit(solution)/shard_map/dot_general | solution.py:116
  389.9 73.1 %reduce-scatter.2.cloned.1.call-done = bf16[24,2560]{1,0:T(8,128)(2,1)} async-done(((bf16[384,2560]{1,0:T(8,128)(2,1)}), bf16[24,2560]{1,0:T(8,128)(2,1)}) %reduce-scatter.2.cloned.1.call-update) | async-done | bytes 122896 | tf_op jit(solution)/shard_map/reduce_scatter | solution.py:122
  463.0 1.6 add_convert_fusion.1
  (85 shorter events, 15.3 us)
Async XLA Ops:
  7.4 183.5 %copy-start = (bf16[256,2560]{1,0:T(8,128)(2,1)S(1)}, bf16[256,2560]{1,0:T(8,128)(2,1)}, u32[]{:S(2)}) copy-start(bf16[256,2560]{1,0:T(8,128)(2,1)} %param.21) | copy-start | bytes 3932164
  8.9 28.8 %all-to-all-start = ((bf16[24,16,128]{2,0,1:T(8,128)(2,1)}), bf16[24,16,128]{2,0,1:T(8,128)(2,1)S(1)}, u32[]{:S(2)}, u32[]{:S(2)}) async-start(bf16[24,16,128]{2,0,1:T(8,128)(2,1)} %bitcast.13), calls=%async_computation | async-start | bytes 196608 | tf_op jit(solution)/shard_map/all_to_all | solution.py:46
  38.4 16.8 %all-to-all-start.1 = ((bf16[24,16,128]{2,0,1:T(8,128)(2,1)}), bf16[24,16,128]{2,0,1:T(8,128)(2,1)S(1)}, u32[]{:S(2)}, u32[]{:S(2)}) async-start(bf16[24,16,128]{2,0,1:T(8,128)(2,1)} %bitcast.23), calls=%async_computation.1 | async-start | bytes 196608 | tf_op jit(solution)/shard_map/all_to_all | solution.py:47
  43.2 16.8 %copy-start.2 = (bf16[1,256,1024]{2,1,0:T(8,128)(2,1)S(1)}, bf16[1,256,1024]{2,1,0:T(8,128)(2,1)}, u32[]{:S(2)}) copy-start(bf16[1,256,1024]{2,1,0:T(8,128)(2,1)} %param.18) | copy-start | bytes 1572868
  56.3 52.6 %all-to-all-start.2 = ((bf16[256,16,128]{2,0,1:T(8,128)(2,1)}), bf16[256,16,128]{2,0,1:T(8,128)(2,1)S(1)}, u32[]{:S(2)}, u32[]{:S(2)}) async-start(bf16[256,16,128]{2,0,1:T(8,128)(2,1)} %bitcast.30), calls=%async_computation.2 | async-start | bytes 2097152 | tf_op jit(solution)/shard_map/all_to_all | solution.py:44
  60.1 58.0 %copy-start.3 = (bf16[384,256]{1,0:T(8,128)(2,1)S(1)}, bf16[384,256]{1,0:T(8,128)(2,1)}, u32[]{:S(2)}) copy-start(bf16[384,256]{1,0:T(8,128)(2,1)} %param.14) | copy-start | bytes 589828
  108.8 1.3 copy-start.1
  110.2 58.0 %all-to-all-start.3 = ((bf16[256,16,128]{2,0,1:T(8,128)(2,1)}), bf16[256,16,128]{2,0,1:T(8,128)(2,1)S(1)}, u32[]{:S(2)}, u32[]{:S(2)}) async-start(bf16[256,16,128]{2,0,1:T(8,128)(2,1)} %bitcast.35), calls=%async_computation.3 | async-start | bytes 2097152 | tf_op jit(solution)/shard_map/all_to_all | solution.py:45
  118.1 215.7 %all-reduce.2.cloned.1.call-start = ((), (), s32[]{:S(2)}) async-start(), calls=%async_computation.5 | async-start | bytes 3932160 | tf_op jit(solution)/shard_map/psum | solution.py:99
  192.9 1.8 copy-start.4
  193.0 143.8 %all-gather.4.cloned.1.call-start = ((), (), s32[]{:S(2)}) async-start(), calls=%async_computation.6 | async-start | bytes 3379200 | tf_op jit(solution)/shard_map/all_gather | solution.py:107
  193.5 148.1 %all-gather.6.cloned.1.call-start = ((), (), s32[]{:S(2)}) async-start(), calls=%async_computation.7 | async-start | bytes 3379200 | tf_op jit(solution)/shard_map/all_gather | solution.py:112
  194.1 187.7 %all-gather.8.cloned.1.call-start = ((), (), s32[]{:S(2)}) async-start(), calls=%async_computation.8 | async-start | bytes 3379200 | tf_op jit(solution)/shard_map/all_gather | solution.py:118
  194.7 268.3 %reduce-scatter.2.cloned.1.call-start = ((), (), s32[]{:S(2)}) async-start(), calls=%async_computation.9 | async-start | bytes 2088960 | tf_op jit(solution)/shard_map/reduce_scatter | solution.py:122
Sparse Core Ops, SparseCore 0:
  193.1 140.6 all-reduce.1
  390.1 72.9 reduce-scatter.1
Sparse Core Ops, SparseCore 1:
  197.1 57.5 all-gather.3
  258.3 59.9 all-gather.5
  321.8 59.9 all-gather.7
where the time goes:
time: 473 us; the launch traced here: 472 us
  waiting for transfers between devices  376 us (79%)
  starting transfers between devices  30.5 us (6%)
  matrix products  30.4 us (6%)
  between operations  15.2 us (3%)
  other arithmetic  12.1 us (3%)
  local copies, waits for them, and re-layouts  7.44 us (2%)
    psum x1, waiting for transfers between devices, shards(): lax.psum(partial_value.astype(jnp.bfloat16), 'mlp').astype(jnp.float32)  139 us
    reduce_scatter x1, waiting for transfers between devices, shards(): lax.psum_scatter(mlp_part.astype(jnp.bfloat16), 'mlp', scatter_dimension=...  73.1 us
    all_to_all x1, waiting for transfers between devices, shards(): lax.all_to_all(to_slots(cache_keys[0]), 'mlp', split_axis=1, concat_axis=...  48.7 us
    all_to_all x1, waiting for transfers between devices, shards(): lax.all_to_all(to_slots(cache_values[0]), 'mlp', split_axis=1, concat_axi...  48.7 us
    all_gather x1, waiting for transfers between devices, shards(): lax.all_gather(down_weight, 'req', axis=0, tiled=True)  40.2 us
    all_to_all x1, starting transfers between devices, shards(): lax.all_to_all(to_slots(new_keys), 'mlp', split_axis=1, concat_axis=0, ti...  15.2 us
    all_to_all x1, waiting for transfers between devices, shards(): lax.all_to_all(to_slots(new_keys), 'mlp', split_axis=1, concat_axis=0, ti...  12.7 us
    all_to_all x1, waiting for transfers between devices, shards(): lax.all_to_all(to_slots(new_values), 'mlp', split_axis=1, concat_axis=0,...  11.9 us
  transfers between devices with their start and end apart: 9, of which 7 were waited for; matrix products, arithmetic and copies ran while one was open for 2% of the time, Pallas kernels for 0%

commit v1 on v0

--- a/solution.py
+++ b/solution.py
@@ -7,6 +7,12 @@
 KVH = 8
 HD = 128
 norm_eps = 1e-06
+
+
+def samples_all_perform(raw):
+    val2 = lax.all_gather(raw, axis_name="mlp")
+    last = jnp.sum(val2, 0)
+    return last
 
 
 def shards(
@@ -96,7 +102,7 @@
     attended = attended.transpose(2, 0, 1, 3).reshape(query_rows, heads_dev * HD)
     partial_value = jnp.dot(attended, out_weight, preferred_element_type=jnp.float32)
     row_start = lax.axis_index("mlp") * rows_dev
-    head_sum = lax.psum(partial_value.astype(jnp.bfloat16), "mlp").astype(jnp.float32)
+    head_sum = samples_all_perform(partial_value.astype(jnp.bfloat16)).astype(jnp.float32)
     stream = (residual.astype(jnp.float32) + head_sum).astype(jnp.bfloat16)
     stream_full = stream.astype(jnp.float32)
     factor = lax.rsqrt(jnp.mean(stream_full * stream_full, axis=-1, keepdims=True) + norm_eps)

time: 473 us -> 805 us (1.70)
  the two profiles are of different devices: /device:TPU:2 before, /device:TPU:6 now
where the time goes in v1:
time: 805 us; the launch traced here: 804 us
  waiting for transfers between devices  697 us (87%)
  matrix products  31.1 us (4%)
  starting transfers between devices  30.7 us (4%)
  other arithmetic  24.1 us (3%)
  between operations  13.4 us (2%)
    all_gather x1, waiting for transfers between devices, samples_all_perform(): val2 = lax.all_gather(raw, axis_name='mlp')  333 us
    reduce_scatter x1, waiting for transfers between devices, shards(): lax.psum_scatter(mlp_part.astype(jnp.bfloat16), 'mlp', scatter_dimension=...  73 us
    all_gather x1, waiting for transfers between devices, shards(): lax.all_gather(up_weight, 'req', axis=0, tiled=True)  63.2 us
    all_gather x1, waiting for transfers between devices, shards(): lax.all_gather(down_weight, 'req', axis=0, tiled=True)  57.9 us
    all_to_all x1, waiting for transfers between devices, shards(): lax.all_to_all(to_slots(cache_keys[0]), 'mlp', split_axis=1, concat_axis=...  48.7 us
    all_to_all x1, waiting for transfers between devices, shards(): lax.all_to_all(to_slots(cache_values[0]), 'mlp', split_axis=1, concat_axi...  48.7 us
    all_gather x1, waiting for transfers between devices, shards(): lax.all_gather(gate_weight, 'req', axis=0, tiled=True)  46.3 us
  transfers between devices with their start and end apart: 9, of which 9 were waited for; matrix products, arithmetic and copies ran while one was open for 3% of the time, Pallas kernels for 0%

profile of v1, /device:TPU:6, one launch (start us, length us, event | category | flops | bytes accessed | tf_op | source)
XLA Modules:
  0.0 804.1 jit_solution(17050621892659843315)
XLA Ops:
  6.5 0.9 copy_bitcast_fusion.1
  8.1 15.2 %all-to-all-start = ((bf16[24,16,128]{2,0,1:T(8,128)(2,1)}), bf16[24,16,128]{2,0,1:T(8,128)(2,1)S(1)}, u32[]{:S(2)}, u32[]{:S(2)}) async-start(bf16[24,16,128]{2,0,1:T(8,128)(2,1)} %bitcast.13), calls=%async_computation | async-start | bytes 196608 | tf_op jit(solution)/shard_map/all_to_all | solution.py:52
  24.1 12.7 %all-to-all-done = bf16[24,16,128]{2,0,1:T(8,128)(2,1)S(1)} async-done(((bf16[24,16,128]{2,0,1:T(8,128)(2,1)}), bf16[24,16,128]{2,0,1:T(8,128)(2,1)S(1)}, u32[]{:S(2)}, u32[]{:S(2)}) %all-to-all-start) | async-done | bytes 98336 | tf_op jit(solution)/shard_map/all_to_all | solution.py:52
  37.5 3.6 all-to-all-start.1
  41.1 1.1 copy.35
  42.3 11.9 %all-to-all-done.1 = bf16[24,16,128]{2,0,1:T(8,128)(2,1)S(1)} async-done(((bf16[24,16,128]{2,0,1:T(8,128)(2,1)}), bf16[24,16,128]{2,0,1:T(8,128)(2,1)S(1)}, u32[]{:S(2)}, u32[]{:S(2)}) %all-to-all-start.1) | async-done | bytes 98336 | tf_op jit(solution)/shard_map/all_to_all | solution.py:53
  54.3 1.2 broadcast_in_dim.98
  55.5 3.7 all-to-all-start.2
  59.3 48.7 %all-to-all-done.2 = bf16[256,16,128]{2,0,1:T(8,128)(2,1)S(1)} async-done(((bf16[256,16,128]{2,0,1:T(8,128)(2,1)}), bf16[256,16,128]{2,0,1:T(8,128)(2,1)S(1)}, u32[]{:S(2)}, u32[]{:S(2)}) %all-to-all-start.2) | async-done | bytes 1048608 | tf_op jit(solution)/shard_map/all_to_all | solution.py:50
  108.0 1.3 broadcast_in_dim.100
  109.3 7.9 all-to-all-start.3
  118.7 48.7 %all-to-all-done.3 = bf16[256,16,128]{2,0,1:T(8,128)(2,1)S(1)} async-done(((bf16[256,16,128]{2,0,1:T(8,128)(2,1)}), bf16[256,16,128]{2,0,1:T(8,128)(2,1)S(1)}, u32[]{:S(2)}, u32[]{:S(2)}) %all-to-all-start.3) | async-done | bytes 1048608 | tf_op jit(solution)/shard_map/all_to_all | solution.py:51
  167.3 22.4 %while.17 = (s32[]{:T(128)}, f32[1,2,384]{2,1,0:T(2,128)S(1)}, f32[1,2,384]{2,1,0:T(2,128)S(1)}, f32[1,2,384,128]{3,2,1,0:T(8,128)S(1)}, s32[]{:T(128)}, /*index...) while((s32[]{:T(128)}, f32[1,2,384]{2,1,0:T(2,128)S(1)}, ...), condition=%wide.region_5.6_spmd, body=%wide.region_2.5_spmd.sunk | while | flops 204279040 | bytes 6014131 | solution.py:100
  168.0 1.3 bitcast_reduce_fusion.2
  170.8 1.3 bitcast_reduce_fusion.2
  173.6 1.3 bitcast_reduce_fusion.2
  176.4 1.3 bitcast_reduce_fusion.2
  179.2 1.3 bitcast_reduce_fusion.2
  182.0 1.3 bitcast_reduce_fusion.2
  184.8 1.3 bitcast_reduce_fusion.2
  187.7 1.3 bitcast_reduce_fusion.2
  190.0 2.0 convolution_convert_fusion.1
  194.4 332.7 %all-gather.12.cloned.1.call-done = bf16[6144,2560]{1,0:T(8,128)(2,1)} async-done(((bf16[384,2560]{1,0:T(8,128)(2,1)}), bf16[6144,2560]{1,0:T(8,128)(2,1)}) %all-gather.12.cloned.1.call-update) | async-done | bytes 31457296 | tf_op jit(solution)/shard_map/all_gather | solution.py:13
  527.0 11.3 %reduce_sum.47 = bf16[384,2560]{1,0:T(8,128)(2,1)S(1)} reduce(bf16[16,384,2560]{2,1,0:T(8,128)(2,1)} %bitcast.148, bf16[]{:T(256)} %constant.68.clone.1), dimensions={0}, to_apply=%region_6.7 | reduce | flops 14745600 | bytes 33423362 | tf_op jit(solution)/shard_map/reduce_sum | solution.py:14
  538.3 3.7 fusion.15
  542.0 46.3 %all-gather.6.cloned.1.call-done = bf16[2560,608]{1,0:T(8,128)(2,1)} async-done(((bf16[80,608]{1,0:T(8,128)(2,1)}), bf16[2560,608]{1,0:T(8,128)(2,1)}) %all-gather.6.cloned.1.call-update) | async-done | bytes 3112976 | tf_op jit(solution)/shard_map/all_gather | solution.py:113
  588.3 5.5 fusion.29
  593.8 57.9 %all-gather.10.cloned.1.call-done = bf16[2560,608]{1,0:T(8,128)(2,1)} async-done(((bf16[80,608]{1,0:T(8,128)(2,1)}), bf16[2560,608]{1,0:T(8,128)(2,1)}) %all-gather.10.cloned.1.call-update) | async-done | bytes 3112976 | tf_op jit(solution)/shard_map/all_gather | solution.py:124
  651.7 63.2 %all-gather.8.cloned.1.call-done = bf16[2560,608]{1,0:T(8,128)(2,1)} async-done(((bf16[80,608]{1,0:T(8,128)(2,1)}), bf16[2560,608]{1,0:T(8,128)(2,1)}) %all-gather.8.cloned.1.call-update) | async-done | bytes 3112976 | tf_op jit(solution)/shard_map/all_gather | solution.py:118
  714.9 8.1 %convolution_convert_fusion = bf16[384,2560]{1,0:T(8,128)(2,1)} fusion(bf16[2560,608]{1,0:T(8,128)(2,1)} %all-gather.10.cloned.1.call-done, bf16[2560,608]{1,0:T(8,128)(2,1)} %all-gather.8.cloned.1.call-done, f32[384,608]{0,1:T(8,128)} %fusion.29, bf16[384,2560]{1,0:T(8,128)(2,1)S(1)} %copy-done.2, f32[2560]{0:T(1024)S(1)} %convert_element_type.59, ...), kind=kOutput, calls=%fused_computation.24 | convolution fusion | flops 2397069312 | bytes 11103744 | tf_op jit(solution)/shard_map/dot_general | solution.py:122
  723.1 73.0 %reduce-scatter.2.cloned.1.call-done = bf16[24,2560]{1,0:T(8,128)(2,1)} async-done(((bf16[384,2560]{1,0:T(8,128)(2,1)}), bf16[24,2560]{1,0:T(8,128)(2,1)}) %reduce-scatter.2.cloned.1.call-update) | async-done | bytes 122896 | tf_op jit(solution)/shard_map/reduce_scatter | solution.py:128
  796.0 1.6 add_convert_fusion.1
  (88 shorter events, 17.9 us)
Async XLA Ops:
  6.5 183.5 %copy-start = (bf16[256,2560]{1,0:T(8,128)(2,1)S(1)}, bf16[256,2560]{1,0:T(8,128)(2,1)}, u32[]{:S(2)}) copy-start(bf16[256,2560]{1,0:T(8,128)(2,1)} %param.21) | copy-start | bytes 3932164
  8.1 28.8 %all-to-all-start = ((bf16[24,16,128]{2,0,1:T(8,128)(2,1)}), bf16[24,16,128]{2,0,1:T(8,128)(2,1)S(1)}, u32[]{:S(2)}, u32[]{:S(2)}) async-start(bf16[24,16,128]{2,0,1:T(8,128)(2,1)} %bitcast.13), calls=%async_computation | async-start | bytes 196608 | tf_op jit(solution)/shard_map/all_to_all | solution.py:52
  37.5 16.8 %all-to-all-start.1 = ((bf16[24,16,128]{2,0,1:T(8,128)(2,1)}), bf16[24,16,128]{2,0,1:T(8,128)(2,1)S(1)}, u32[]{:S(2)}, u32[]{:S(2)}) async-start(bf16[24,16,128]{2,0,1:T(8,128)(2,1)} %bitcast.23), calls=%async_computation.1 | async-start | bytes 196608 | tf_op jit(solution)/shard_map/all_to_all | solution.py:53
  42.3 16.8 %copy-start.3 = (bf16[1,256,1024]{2,1,0:T(8,128)(2,1)S(1)}, bf16[1,256,1024]{2,1,0:T(8,128)(2,1)}, u32[]{:S(2)}) copy-start(bf16[1,256,1024]{2,1,0:T(8,128)(2,1)} %param.18) | copy-start | bytes 1572868
  55.5 52.6 %all-to-all-start.2 = ((bf16[256,16,128]{2,0,1:T(8,128)(2,1)}), bf16[256,16,128]{2,0,1:T(8,128)(2,1)S(1)}, u32[]{:S(2)}, u32[]{:S(2)}) async-start(bf16[256,16,128]{2,0,1:T(8,128)(2,1)} %bitcast.30), calls=%async_computation.2 | async-start | bytes 2097152 | tf_op jit(solution)/shard_map/all_to_all | solution.py:50
  59.3 58.0 %copy-start.4 = (bf16[384,256]{1,0:T(8,128)(2,1)S(1)}, bf16[384,256]{1,0:T(8,128)(2,1)}, u32[]{:S(2)}) copy-start(bf16[384,256]{1,0:T(8,128)(2,1)} %param.14) | copy-start | bytes 589828
  108.0 1.3 copy-start.1
  109.3 58.0 %all-to-all-start.3 = ((bf16[256,16,128]{2,0,1:T(8,128)(2,1)}), bf16[256,16,128]{2,0,1:T(8,128)(2,1)S(1)}, u32[]{:S(2)}, u32[]{:S(2)}) async-start(bf16[256,16,128]{2,0,1:T(8,128)(2,1)} %bitcast.35), calls=%async_computation.3 | async-start | bytes 2097152 | tf_op jit(solution)/shard_map/all_to_all | solution.py:51
  117.2 409.8 %all-gather.12.cloned.1.call-start = ((), (), s32[]{:S(2)}) async-start(), calls=%async_computation.9 | async-start | bytes 33423360 | tf_op jit(solution)/shard_map/all_gather | solution.py:13
  192.0 2.3 copy-start.5
  192.0 396.3 %all-gather.6.cloned.1.call-start = ((), (), s32[]{:S(2)}) async-start(), calls=%async_computation.5 | async-start | bytes 3379200 | tf_op jit(solution)/shard_map/all_gather | solution.py:113
  192.8 458.9 %all-gather.10.cloned.1.call-start = ((), (), s32[]{:S(2)}) async-start(), calls=%async_computation.7 | async-start | bytes 3379200 | tf_op jit(solution)/shard_map/all_gather | solution.py:124
  193.5 521.4 %all-gather.8.cloned.1.call-start = ((), (), s32[]{:S(2)}) async-start(), calls=%async_computation.6 | async-start | bytes 3379200 | tf_op jit(solution)/shard_map/all_gather | solution.py:118
  194.1 601.9 %reduce-scatter.2.cloned.1.call-start = ((), (), s32[]{:S(2)}) async-start(), calls=%async_computation.8 | async-start | bytes 2088960 | tf_op jit(solution)/shard_map/reduce_scatter | solution.py:128
  588.3 126.6 %copy-start.2 = (bf16[384,2560]{1,0:T(8,128)(2,1)S(1)}, bf16[384,2560]{1,0:T(8,128)(2,1)}, u32[]{:S(2)}) copy-start(bf16[384,2560]{1,0:T(8,128)(2,1)} %get-tuple-element.174) | copy-start | bytes 5898244
Sparse Core Ops, SparseCore 0:
  192.2 334.8 all-gather.11
  530.2 58.0 all-gather.5
  591.5 60.1 all-gather.9
  654.7 60.1 all-gather.7
  723.2 72.8 reduce-scatter.1
